TPU v7x, 256 devices: a whole 4x4x8 slice. The times are simulated.
256 devices in a mesh: leaf: 2 (over core), row: 8 (over z), col: 16 (over y, x).
Axes of the slice: x: 4, y: 4, z: 8, core: 2. Of those that a mesh axis runs over, the one named last changes fastest.
Arguments:
- front: float32 [2, 8, 8, 128, 4, 16, 128], P('leaf', None, 'row', None, None, 'col'), as said below
- parent: float32 [4, 2, 8, 128, 4, 16, 128], P(None, 'leaf', 'row', None, None, 'col'), may hold values from -0.2 to 0.2
- tile_map: int32 [2, 56], replicated, may hold values from 0 to 63, as said below
- col_shift: int32 [4], replicated, may hold values from 0 to 7
Outputs:
- factored: float32 [2, 8, 8, 128, 4, 16, 128], P('leaf', None, 'row', None, None, 'col')
- new_parent: float32 [4, 2, 8, 128, 4, 16, 128], P(None, 'leaf', 'row', None, None, 'col')
Inputs may be any that keep to these rules, and one draw needn't show every extreme that they name: For each leaf the 8192 x 8192 matrix read from front is symmetric positive definite. Entry [l, e] names the parent tile joined by tile 8 + e of child l; no row repeats a value. The parent tile q = tile_map[l, e] has (q mod 16 + col_shift[q // 16]) mod 16 equal to (8 + e) mod 16. Among the tiles of one child whose indices are equal mod 8, at most 1 have parent tiles equal mod 16.
All inputs are finite; a program needn't handle non-finite values.
Results may differ from a plain program's by a relative error of at most 0.0001.
Values sent between devices are 32-bit elements; how exact they have to be, the bound alone decides.
No kernel may reach another device: no remote copies, remote signals or barrier semaphores. Data moves between devices by JAX's collectives and lax.ppermute only.
A program may use at most 128 MiB of HBM per device.

v0:
```python
import jax
import jax.numpy as jnp
from jax import lax
from jax.sharding import PartitionSpec as P

TILE = 128
PB = 512
PANELS = 2
NPIV = 1024
HIGHEST = lax.Precision.HIGHEST


def spread(value, axis, source):
    kept = jnp.where(lax.axis_index(axis) == source, value, 0).astype(value.dtype)
    return lax.psum(kept, axis)


def update_slots(working, next_rows, column_factor, slot_low, slot_high):
    product = jnp.einsum(
        "atp,bsp->atbs",
        next_rows,
        column_factor,
        precision=HIGHEST,
        preferred_element_type=jnp.float32,
    )
    return working.at[:, :, slot_low:slot_high, :].add(-product)


def per_device(front, parent, tile_map, col_shift):
    leaf_count = lax.axis_size("leaf")
    row_count = lax.axis_size("row")
    col_count = lax.axis_size("col")
    leaf_index = lax.axis_index("leaf")
    row_index = lax.axis_index("row")
    col_index = lax.axis_index("col")
    local_front = front[0, :, 0, :, :, 0, :]
    row_slots = local_front.shape[0]
    col_slots = local_front.shape[2]
    panel_tiles = PB // TILE
    pivot_tiles = NPIV // TILE
    row_tiles = jnp.arange(row_slots, dtype=jnp.int32) * row_count + row_index
    col_tiles = jnp.arange(col_slots, dtype=jnp.int32) * col_count + col_index

    def fetch_panel(working, panel_index):
        pieces = []
        for offset in range(panel_tiles):
            column = panel_index * panel_tiles + offset
            column_tile = working[:, :, column // col_count, :]
            pieces.append(spread(column_tile, "col", column % col_count))
        return jnp.concatenate(pieces, axis=2)

    def write_factor(working, factor, panel_index):
        first_column = panel_index * panel_tiles
        slot_values = sorted(
            set([(first_column + offset) // col_count for offset in range(panel_tiles)])
        )
        for slot_index in slot_values:
            current = working[:, :, slot_index, :]
            for offset in range(panel_tiles):
                column = first_column + offset
                if column // col_count == slot_index:
                    current = jnp.where(
                        col_index == column % col_count,
                        factor[:, :, offset * TILE : (offset + 1) * TILE],
                        current,
                    )
            working = working.at[:, :, slot_index, :].set(current)
        return working

    working = local_front
    panel_block = fetch_panel(working, 0)
    for panel_index in range(PANELS):
        first_tile = panel_index * panel_tiles
        factor_slot_index = first_tile // row_count
        start_row = first_tile % row_count
        gathered = lax.all_gather(panel_block[factor_slot_index], "row", axis=0, tiled=True)
        diagonal_block = gathered[start_row * TILE : (start_row + panel_tiles) * TILE]
        lower_factor = jnp.linalg.cholesky(diagonal_block)
        factor_flattened = panel_block.reshape(row_slots * TILE, PB)
        solved = lax.linalg.triangular_solve(
            lower_factor, factor_flattened, left_side=False, lower=True, transpose_a=True
        )
        solved = solved.reshape(row_slots, TILE, PB)
        offset_tile = jnp.clip(row_index - start_row, 0, panel_tiles - 1)
        diagonal_rows = lax.dynamic_slice_in_dim(lower_factor, offset_tile * TILE, TILE, 0)
        in_panel = (row_tiles >= first_tile) & (row_tiles < first_tile + panel_tiles)
        factor_factor = jnp.where(in_panel[:, None, None], diagonal_rows[None], solved)
        factor_factor = jnp.where((row_tiles >= first_tile)[:, None, None], factor_factor, 0.0)
        next_rows = jnp.where(
            (row_tiles >= first_tile + panel_tiles)[:, None, None], factor_factor, 0.0
        )
        group_size = col_count // row_count
        owner_rows = spread(next_rows, "row", col_index % row_count)
        grouped = owner_rows.reshape(col_slots, group_size, TILE, PB)
        column_factor = lax.dynamic_index_in_dim(grouped, col_index // row_count, 1, keepdims=False)
        column_factor = jnp.where(
            (col_tiles >= first_tile + panel_tiles)[:, None, None], column_factor, 0.0
        )
        factor, next_rows, column_factor = (factor_factor, next_rows, column_factor)
        working = update_slots(working, next_rows, column_factor, 0, col_slots)
        upcoming = (
            fetch_panel(working, panel_index + 1) if panel_index + 1 < PANELS else panel_block
        )
        working = write_factor(working, factor, panel_index)
        panel_block = upcoming
    upper_part = (row_tiles < pivot_tiles)[:, None, None, None] & (col_tiles >= pivot_tiles)[
        None, None, :, None
    ]
    working = jnp.where(upper_part, 0.0, working)
    factored = working.reshape(front.shape)
    contribution = jnp.where((col_tiles >= pivot_tiles)[None, None, :, None], working, 0.0)
    contrib_count = tile_map.shape[1]
    entry_ids = jnp.arange(contrib_count, dtype=jnp.int32)
    own_map = lax.dynamic_index_in_dim(tile_map, leaf_index, 0, keepdims=False)
    row_match = (row_tiles - pivot_tiles)[:, None] == entry_ids[None, :]
    row_targets = jnp.sum(jnp.where(row_match, own_map[None, :], 0), axis=1)
    row_valid = row_tiles >= pivot_tiles
    owner_count = leaf_count * row_count
    destination = row_targets % owner_count
    parent_row_slot = row_targets // owner_count
    slot_ids = jnp.arange(row_slots, dtype=jnp.int32)
    same_before = (
        (destination[None, :] == destination[:, None])
        & row_valid[None, :]
        & (slot_ids[None, :] < slot_ids[:, None])
    )
    rank_in_dest = jnp.sum(same_before.astype(jnp.int32), axis=1)
    capacity = (col_slots + row_count - 1) // row_count
    owner_ids = jnp.arange(owner_count, dtype=jnp.int32)
    capacity_ids = jnp.arange(capacity, dtype=jnp.int32)
    selection = (
        row_valid[None, None, :]
        & (destination[None, None, :] == owner_ids[:, None, None])
        & (rank_in_dest[None, None, :] == capacity_ids[None, :, None])
    )
    flattened = contribution.reshape(row_slots, -1)
    send_buffer = jnp.einsum(
        "oka,ax->okx",
        selection.astype(jnp.float32),
        flattened,
        precision=HIGHEST,
        preferred_element_type=jnp.float32,
    )
    chosen_slot = jnp.sum(jnp.where(selection, parent_row_slot[None, None, :], 0), axis=2)
    send_slots = jnp.where(jnp.any(selection, axis=2), chosen_slot, -1)
    received, received_slots = (
        lax.all_to_all(send_buffer, ("leaf", "row"), split_axis=0, concat_axis=0, tiled=True),
        lax.all_to_all(send_slots, ("leaf", "row"), split_axis=0, concat_axis=0, tiled=True),
    )
    received = received.reshape(leaf_count, row_count, capacity, -1)
    received_slots = received_slots.reshape(leaf_count, row_count, capacity)
    parent_local = parent[:, 0, 0, :, :, 0, :]
    parent_rows = parent_local.shape[0]
    parent_cols = parent_local.shape[2]
    row_place = (
        received_slots[None] == jnp.arange(parent_rows, dtype=jnp.int32)[:, None, None, None]
    ).astype(jnp.float32)
    by_leaf = jnp.einsum(
        "slrk,lrkx->slx", row_place, received, precision=HIGHEST, preferred_element_type=jnp.float32
    )
    by_leaf = by_leaf.reshape(parent_rows, leaf_count, TILE, col_slots, TILE)
    col_match = (col_tiles - pivot_tiles)[:, None] == entry_ids[None, :]
    col_targets = jnp.sum(jnp.where(col_match[None], tile_map[:, None, :], 0), axis=2)
    col_valid = col_tiles >= pivot_tiles
    parent_slot_ids = jnp.arange(parent_cols, dtype=jnp.int32)
    col_place = (
        col_valid[None, None, :]
        & (col_targets[:, None, :] // col_count == parent_slot_ids[None, :, None])
    ).astype(jnp.float32)
    assembled = jnp.einsum(
        "sltbv,lub->stuv", by_leaf, col_place, precision=HIGHEST, preferred_element_type=jnp.float32
    )
    new_parent = (parent_local + assembled).reshape(parent.shape)
    return (factored, new_parent)


def solution(mesh):
    return jax.shard_map(
        per_device,
        mesh=mesh,
        in_specs=(
            P("leaf", None, "row", None, None, "col", None),
            P(None, "leaf", "row", None, None, "col", None),
            P(),
            P(),
        ),
        out_specs=(
            P("leaf", None, "row", None, None, "col", None),
            P(None, "leaf", "row", None, None, "col", None),
        ),
        check_vma=False,
    )
```

profile of v0, /device:TPU:1, one launch (start us, length us, event | category | flops | bytes accessed | tf_op | source)
XLA Modules:
  0.0 995.7 jit_solution(4092188100553603286)
XLA Ops:
  7.2 4.6 copy.98
  13.8 103.2 %all-reduce.14.cloned.1.call-done = (f32[8,128,128]{1,2,0:T(8,128)}, f32[8,128,128]{1,2,0:T(8,128)}, f32[8,128,128]{1,2,0:T(8,128)}, f32[8,128,128]{1,2,0:T(8,128)}) async-done(((f32[8,128,128]{1,2,0:T(8,128)}, f32[8,128,128]{1,2,0:T(8,128)}, f32[8,128,128]{1,2,0:T(8,128)}, f32[8,128,128]{1,2,0:T(8,128)}), (f32[8,128,128]{1,2,0:T(8,128)}, f32[8,128,128]{1,2,0:T(8,128)}, f32[8,128,128]{1,2,0:T(8,128)}, ...) | async-done | bytes 2097168 | tf_op jit(solution)/shard_map/psum | solution.py:15
  124.1 41.6 %all-gather.5.cloned.1.call-done = f32[1,1024,512]{1,2,0:T(8,128)} async-done(((f32[1,128,512]{1,2,0:T(8,128)}), f32[1,1024,512]{1,2,0:T(8,128)}) %all-gather.5.cloned.1.call-update) | async-done | bytes 2097168 | tf_op jit(solution)/shard_map/all_gather | solution.py:76
  172.0 11.7 %cholesky.286 = f32[128,128]{1,0:T(8,128)S(1)} custom-call(f32[128,128]{1,0:T(8,128)S(1)} %cholesky.426), custom_call_target="Cholesky" | custom-call | tf_op jit(solution)/shard_map/jit(cholesky)/cholesky | solution.py:78
  183.8 9.8 custom-call.27
  196.2 11.7 %cholesky.305 = f32[128,128]{1,0:T(8,128)S(1)} custom-call(f32[128,128]{1,0:T(8,128)S(1)} %cholesky.430), custom_call_target="Cholesky" | custom-call | tf_op jit(solution)/shard_map/jit(cholesky)/cholesky | solution.py:78
  207.9 10.0 custom-call.28
  219.5 11.7 %cholesky.326 = f32[128,128]{1,0:T(8,128)S(1)} custom-call(f32[128,128]{1,0:T(8,128)S(1)} %cholesky.435), custom_call_target="Cholesky" | custom-call | tf_op jit(solution)/shard_map/jit(cholesky)/cholesky | solution.py:78
  231.2 9.8 custom-call.29
  242.5 11.7 %cholesky.343 = f32[128,128]{1,0:T(8,128)S(1)} custom-call(f32[128,128]{1,0:T(8,128)S(1)} %convolution_subtract_fusion.9), custom_call_target="Cholesky" | custom-call | tf_op jit(solution)/shard_map/jit(cholesky)/cholesky | solution.py:78
  260.8 11.7 %while.10 = (s32[]{:T(128)}, f32[512,512]{1,0:T(8,128)}, s32[4,2]{0,1:T(2,128)S(1)}, f32[4,128,128]{2,1,0:T(8,128)S(1)}, s32[]{:T(128)}) while((s32[]{:T(128)}, f32[512,512]{1,0:T(8,128)}, s32[4,2]{0,1:T(2,128)S(1)}, f32[4,128,128]{2,1,0:T(8,128)S(1)}, s32[]{:T(128)}) %tuple.99), condition=%wide.while_cond.4, body=%wide.while_body.4.sunk | while | flops 2 | bytes 131189 | solution.py:80
  272.5 39.3 %custom-call.30 = f32[4,128,128]{1,2,0:T(8,128)S(1)} custom-call(f32[4,128,128]{2,1,0:T(8,128)S(1)} %get-tuple-element.82), custom_call_target="InvertDiagBlocksLowerTriangular" | custom-call | tf_op jit(solution)/shard_map/triangular_solve/custom-call.3 | solution.py:80
  318.3 3.8 fusion.18
  327.4 3.9 pad_maximum_fusion
  331.2 2.9 copy.104
  334.2 2.9 copy.105
  337.1 4.0 select_select_fusion.3
  346.0 79.9 %all-reduce.8.cloned.1.call-done = f32[4,2,128,512]{3,2,0,1:T(8,128)} async-done(((f32[4,2,128,512]{3,2,0,1:T(8,128)}), f32[4,2,128,512]{3,2,0,1:T(8,128)}) %all-reduce.8.cloned.1.call-update) | async-done | bytes 2097168 | tf_op jit(solution)/shard_map/psum | solution.py:15
  425.9 5.8 negate_add_fusion.1
  433.2 101.6 %all-reduce.12.cloned.1.call-done = (f32[8,128,128]{1,2,0:T(8,128)}, f32[8,128,128]{1,2,0:T(8,128)}, f32[8,128,128]{1,2,0:T(8,128)}, f32[8,128,128]{1,2,0:T(8,128)}) async-done(((f32[8,128,128]{1,2,0:T(8,128)}, f32[8,128,128]{1,2,0:T(8,128)}, f32[8,128,128]{1,2,0:T(8,128)}, f32[8,128,128]{1,2,0:T(8,128)}), (f32[8,128,128]{1,2,0:T(8,128)}, f32[8,128,128]{1,2,0:T(8,128)}, f32[8,128,128]{1,2,0:T(8,128)}, ...) | async-done | bytes 2097168 | tf_op jit(solution)/shard_map/psum | solution.py:15
  539.3 3.0 copy.112
  542.4 41.1 %all-gather.7.cloned.1.call-done = f32[1,1024,512]{1,2,0:T(8,128)} async-done(((f32[1,128,512]{1,2,0:T(8,128)}), f32[1,1024,512]{1,2,0:T(8,128)}) %all-gather.7.cloned.1.call-update) | async-done | bytes 2097168 | tf_op jit(solution)/shard_map/all_gather | solution.py:76
  589.7 11.7 %cholesky.358 = f32[128,128]{1,0:T(8,128)S(1)} custom-call(f32[128,128]{1,0:T(8,128)S(1)} %cholesky.439), custom_call_target="Cholesky" | custom-call | tf_op jit(solution)/shard_map/jit(cholesky)/cholesky | solution.py:78
  601.6 9.8 custom-call.31
  614.0 11.7 %cholesky.377 = f32[128,128]{1,0:T(8,128)S(1)} custom-call(f32[128,128]{1,0:T(8,128)S(1)} %cholesky.443), custom_call_target="Cholesky" | custom-call | tf_op jit(solution)/shard_map/jit(cholesky)/cholesky | solution.py:78
  625.7 10.0 %custom-call.32 = f32[1,128,128]{1,2,0:T(8,128)S(1)} custom-call(f32[1,128,128]{2,1,0:T(8,128)S(1)} %get-tuple-element.150), custom_call_target="InvertDiagBlocksLowerTriangular" | custom-call | tf_op jit(solution)/shard_map/jit(cholesky)/cholesky | solution.py:78
  637.3 11.7 %cholesky.398 = f32[128,128]{1,0:T(8,128)S(1)} custom-call(f32[128,128]{1,0:T(8,128)S(1)} %cholesky.448), custom_call_target="Cholesky" | custom-call | tf_op jit(solution)/shard_map/jit(cholesky)/cholesky | solution.py:78
  649.0 9.8 custom-call.33
  660.3 11.7 %cholesky.415 = f32[128,128]{1,0:T(8,128)S(1)} custom-call(f32[128,128]{1,0:T(8,128)S(1)} %convolution_subtract_fusion.8), custom_call_target="Cholesky" | custom-call | tf_op jit(solution)/shard_map/jit(cholesky)/cholesky | solution.py:78
  679.1 11.4 %while.11 = (s32[]{:T(128)}, f32[512,512]{1,0:T(8,128)}, s32[4,2]{0,1:T(2,128)S(1)}, f32[4,128,128]{2,1,0:T(8,128)S(1)}, s32[]{:T(128)}) while((s32[]{:T(128)}, f32[512,512]{1,0:T(8,128)}, s32[4,2]{0,1:T(2,128)S(1)}, f32[4,128,128]{2,1,0:T(8,128)S(1)}, s32[]{:T(128)}) %tuple.119), condition=%wide.while_cond.4.clone, body=%wide.while_body.4.clone.sunk | while | flops 2 | bytes 131189 | solution.py:80
  690.5 39.3 %custom-call.34 = f32[4,128,128]{1,2,0:T(8,128)S(1)} custom-call(f32[4,128,128]{2,1,0:T(8,128)S(1)} %get-tuple-element.83), custom_call_target="InvertDiagBlocksLowerTriangular" | custom-call | tf_op jit(solution)/shard_map/triangular_solve/custom-call.3 | solution.py:80
  737.7 3.8 fusion.15
  746.3 3.0 copy.113
  749.3 4.8 pad_maximum_fusion.1
  757.0 3.1 copy.115
  760.1 4.0 select_select_fusion
  767.9 9.3 all-to-all-start.1
  781.9 67.1 %all-reduce.10.cloned.1.call-done = f32[4,2,128,512]{3,2,0,1:T(8,128)} async-done(((f32[4,2,128,512]{3,2,0,1:T(8,128)}), f32[4,2,128,512]{3,2,0,1:T(8,128)}) %all-reduce.10.cloned.1.call-update) | async-done | bytes 2097168 | tf_op jit(solution)/shard_map/psum | solution.py:15
  849.1 5.6 negate_add_fusion
  856.8 3.1 copy.119
  859.9 3.9 reshape.731
  863.8 3.5 convolution_bitcast_fusion
  867.3 6.3 copy.120
  873.6 8.6 all-to-all-start
  882.9 3.6 copy.123
  886.5 88.3 %all-to-all-done = f32[16,1,65536]{2,1,0:T(1,128)} async-done(((f32[16,1,65536]{2,1,0:T(1,128)}), f32[16,1,65536]{2,1,0:T(1,128)}, u32[]{:S(2)}, u32[]{:S(2)}) %all-to-all-start) | async-done | bytes 4194336 | tf_op jit(solution)/shard_map/all_to_all | solution.py:147
  974.8 7.8 convolution_bitcast_fusion.1
  982.6 3.1 reshape.733
  (187 shorter events, 115.7 us)
Async XLA Ops:
  7.2 109.8 %all-reduce.14.cloned.1.call-start = ((), (), s32[]{:S(2)}) async-start(), calls=%async_computation.7 | async-start | bytes 4194304 | tf_op jit(solution)/shard_map/psum | solution.py:15
  11.8 2.0 copy-start
  13.8 151.9 %all-gather.5.cloned.1.call-start = ((), (), s32[]{:S(2)}) async-start(), calls=%async_computation.4 | async-start | bytes 2359296 | tf_op jit(solution)/shard_map/all_gather | solution.py:76
  117.0 2.3 copy-start.14
  117.0 2.3 copy-start.12
  118.1 3.4 copy-start.16
  119.3 1.3 copy-start.5
  121.4 304.5 %all-reduce.8.cloned.1.call-start = ((), (), s32[]{:S(2)}) async-start(), calls=%async_computation.2 | async-start | bytes 4194304 | tf_op jit(solution)/shard_map/psum | solution.py:15
  171.0 1.0 copy-start.7
  318.3 3.8 copy-start.4
  334.2 2.9 copy-start.11
  344.1 190.7 %all-reduce.12.cloned.1.call-start = ((), (), s32[]{:S(2)}) async-start(), calls=%async_computation.6 | async-start | bytes 4194304 | tf_op jit(solution)/shard_map/psum | solution.py:15
  433.1 150.4 %all-gather.7.cloned.1.call-start = ((), (), s32[]{:S(2)}) async-start(), calls=%async_computation.5 | async-start | bytes 2359296 | tf_op jit(solution)/shard_map/all_gather | solution.py:76
  534.8 2.3 copy-start.15
  534.8 2.3 copy-start.13
  537.1 1.3 copy-start.6
  539.2 309.9 %all-reduce.10.cloned.1.call-start = ((), (), s32[]{:S(2)}) async-start(), calls=%async_computation.3 | async-start | bytes 4194304 | tf_op jit(solution)/shard_map/psum | solution.py:15
  588.8 1.0 copy-start.8
  729.8 4.6 copy-start.1
  737.7 3.8 copy-start.3
  757.0 3.1 copy-start.10
  767.9 105.7 %all-to-all-start.1 = ((s32[16,1,1]{2,1,0:T(1,128)}), s32[16,1,1]{2,1,0:T(1,128)S(1)}, u32[]{:S(2)}, u32[]{:S(2)}) async-start(s32[16,1,1]{2,1,0:T(1,128)} %copy.121), calls=%async_computation.1 | async-start | bytes 16384 | tf_op jit(solution)/shard_map/all_to_all | solution.py:148
  849.1 5.7 copy-start.2
  873.6 101.2 %all-to-all-start = ((f32[16,1,65536]{2,1,0:T(1,128)}), f32[16,1,65536]{2,1,0:T(1,128)}, u32[]{:S(2)}, u32[]{:S(2)}) async-start(f32[16,1,65536]{2,1,0:T(1,128)} %copy.120), calls=%async_computation | async-start | bytes 8388608 | tf_op jit(solution)/shard_map/all_to_all | solution.py:147
  982.6 3.1 copy-start.9
Sparse Core Ops, SparseCore 0:
  13.5 103.4 all-reduce.13
  121.5 44.1 all-gather.4
  344.2 81.6 all-reduce.7
  433.2 101.4 all-reduce.11
  539.3 44.1 all-gather.6
  767.2 81.8 all-reduce.9
where the time goes:
time: 1010 us; the launch traced here: 996 us
  waiting for transfers between devices  523 us (52%)
  other arithmetic  267 us (26%)
  local copies, waits for them, and re-layouts  105 us (10%)
  matrix products  61.2 us (6%)
  between operations  21 us (2%)
  starting transfers between devices  18.2 us (2%)
    psum x4, waiting for transfers between devices, spread(): return lax.psum(kept, axis)  352 us
    another operation x29, other arithmetic, per_device(): lower_factor = jnp.linalg.cholesky(diagonal_block)  158 us
    another operation x7, other arithmetic, per_device(): lax.linalg.triangular_solve(lower_factor, factor_flattened, left_side=Fal...  90.5 us
    all_to_all x1, waiting for transfers between devices, per_device(): lax.all_to_all(send_buffer, ('leaf', 'row'), split_axis=0, concat_axis=0,...  88.3 us
    all_gather x2, waiting for transfers between devices, per_device(): lax.all_gather(panel_block[factor_slot_index], 'row', axis=0, tiled=True)  82.7 us
    another operation x29, local copies, waits for them, and re-layouts, per_device(): lax.linalg.triangular_solve(lower_factor, factor_flattened, left_side=Fal...  28.8 us
    another operation x14, matrix products, per_device(): lax.linalg.triangular_solve(lower_factor, factor_flattened, left_side=Fal...  24.7 us
  transfers between devices with their start and end apart: 8, of which 7 were waited for; matrix products, arithmetic and copies ran while one was open for 4% of the time, Pallas kernels for 0%

commit v1 on v0

--- a/solution.py
+++ b/solution.py
@@ -73,7 +73,37 @@
         first_tile = panel_index * panel_tiles
         factor_slot_index = first_tile // row_count
         start_row = first_tile % row_count
-        gathered = lax.all_gather(panel_block[factor_slot_index], "row", axis=0, tiled=True)
+        devices, position, rows = (
+            lax.axis_size("row"),
+            lax.axis_index("row"),
+            panel_block[factor_slot_index].shape[0],
+        )
+        ahead = [(i, (i + 1) % devices) for i in range(devices)]
+        left = [(i, (i - 1) % devices) for i in range(devices)]
+        whole = jnp.zeros(
+            (
+                *panel_block[factor_slot_index].shape[:0],
+                devices * rows,
+                *panel_block[factor_slot_index].shape[0 + 1 :],
+            ),
+            panel_block[factor_slot_index].dtype,
+        )
+        whole = lax.dynamic_update_slice_in_dim(
+            whole, panel_block[factor_slot_index], position * rows, axis=0
+        )
+        from_left = from_right = panel_block[factor_slot_index]
+        middle = devices // 2
+        for lap in range(1, middle + 1):
+            from_left = lax.ppermute(from_left, "row", ahead)
+            whole = lax.dynamic_update_slice_in_dim(
+                whole, from_left, (position - lap) % devices * rows, axis=0
+            )
+            if lap < devices - middle:
+                from_right = lax.ppermute(from_right, "row", left)
+                whole = lax.dynamic_update_slice_in_dim(
+                    whole, from_right, (position + lap) % devices * rows, axis=0
+                )
+        gathered = whole
         diagonal_block = gathered[start_row * TILE : (start_row + panel_tiles) * TILE]
         lower_factor = jnp.linalg.cholesky(diagonal_block)
         factor_flattened = panel_block.reshape(row_slots * TILE, PB)

time: 1010 us -> 970 us (0.960)
  waiting for transfers between devices: 523 us -> 463 us
  starting transfers between devices: 18.2 us -> 38.5 us
    all_gather x2 -> x0, waiting for transfers between devices: 82.7 us -> none  [per_device(): lax.all_gather(panel_block[factor_slot_index], 'row', axis=0, tiled=True)]
    ppermute x0 -> x14, waiting for transfers between devices: none -> 25 us  [the longest x8 25 us: per_device(): from_left = lax.ppermute(from_left, 'row', ahead)]
    ppermute x0 -> x14, starting transfers between devices: none -> 17.9 us  [the longest x6 14.5 us: per_device(): from_right = lax.ppermute(from_right, 'row', left)]
  transfers between devices with their start and end apart: 8 -> 20, of which waited for: 7 -> 11; matrix products, arithmetic and copies ran while one was open for 4% -> 5% of each run, Pallas kernels for 0% -> 0%
where the time goes in v1:
time: 970 us; the launch traced here: 963 us
  waiting for transfers between devices  463 us (48%)
  other arithmetic  266 us (27%)
  local copies, waits for them, and re-layouts  113 us (12%)
  matrix products  61.2 us (6%)
  starting transfers between devices  38.5 us (4%)
  between operations  19.9 us (2%)
    psum x4, waiting for transfers between devices, spread(): return lax.psum(kept, axis)  350 us
    another operation x29, other arithmetic, per_device(): lower_factor = jnp.linalg.cholesky(diagonal_block)  158 us
    another operation x7, other arithmetic, per_device(): lax.linalg.triangular_solve(lower_factor, factor_flattened, left_side=Fal...  90.5 us
    all_to_all x1, waiting for transfers between devices, per_device(): lax.all_to_all(send_buffer, ('leaf', 'row'), split_axis=0, concat_axis=0,...  88.3 us
    another operation x29, local copies, waits for them, and re-layouts, per_device(): lax.linalg.triangular_solve(lower_factor, factor_flattened, left_side=Fal...  28.3 us
    ppermute x8, waiting for transfers between devices, per_device(): from_left = lax.ppermute(from_left, 'row', ahead)  25 us
    another operation x14, matrix products, per_device(): lax.linalg.triangular_solve(lower_factor, factor_flattened, left_side=Fal...  24.7 us
  transfers between devices with their start and end apart: 20, of which 11 were waited for; matrix products, arithmetic and copies ran while one was open for 5% of the time, Pallas kernels for 0%

profile of v1, /device:TPU:1, one launch (start us, length us, event | category | flops | bytes accessed | tf_op | source)
XLA Modules:
  0.0 962.7 jit_solution(14400544163648837180)
XLA Ops:
  7.2 4.6 copy.98
  13.9 103.0 %all-reduce.14.cloned.1.call-done = (f32[8,128,128]{1,2,0:T(8,128)}, f32[8,128,128]{1,2,0:T(8,128)}, f32[8,128,128]{1,2,0:T(8,128)}, f32[8,128,128]{1,2,0:T(8,128)}) async-done(((f32[8,128,128]{1,2,0:T(8,128)}, f32[8,128,128]{1,2,0:T(8,128)}, f32[8,128,128]{1,2,0:T(8,128)}, f32[8,128,128]{1,2,0:T(8,128)}), (f32[8,128,128]{1,2,0:T(8,128)}, f32[8,128,128]{1,2,0:T(8,128)}, f32[8,128,128]{1,2,0:T(8,128)}, ...) | async-done | bytes 2097168 | tf_op jit(solution)/shard_map/psum | solution.py:15
  124.0 4.7 collective-permute-done
  138.4 3.6 collective-permute-done.4
  142.7 6.3 collective-permute-done.6
  152.8 11.7 %cholesky.286 = f32[128,128]{1,0:T(8,128)S(1)} custom-call(f32[128,128]{1,0:T(8,128)S(1)} %cholesky.426), custom_call_target="Cholesky" | custom-call | tf_op jit(solution)/shard_map/jit(cholesky)/cholesky | solution.py:108
  164.7 9.8 %custom-call.27 = f32[1,128,128]{1,2,0:T(8,128)S(1)} custom-call(f32[1,128,128]{2,1,0:T(8,128)S(1)} %get-tuple-element.163), custom_call_target="InvertDiagBlocksLowerTriangular" | custom-call | tf_op jit(solution)/shard_map/jit(cholesky)/cholesky | solution.py:108
  177.1 11.7 %cholesky.305 = f32[128,128]{1,0:T(8,128)S(1)} custom-call(f32[128,128]{1,0:T(8,128)S(1)} %cholesky.430), custom_call_target="Cholesky" | custom-call | tf_op jit(solution)/shard_map/jit(cholesky)/cholesky | solution.py:108
  188.8 10.0 %custom-call.28 = f32[1,128,128]{1,2,0:T(8,128)S(1)} custom-call(f32[1,128,128]{2,1,0:T(8,128)S(1)} %get-tuple-element.160), custom_call_target="InvertDiagBlocksLowerTriangular" | custom-call | tf_op jit(solution)/shard_map/jit(cholesky)/cholesky | solution.py:108
  200.3 11.7 %cholesky.326 = f32[128,128]{1,0:T(8,128)S(1)} custom-call(f32[128,128]{1,0:T(8,128)S(1)} %cholesky.435), custom_call_target="Cholesky" | custom-call | tf_op jit(solution)/shard_map/jit(cholesky)/cholesky | solution.py:108
  212.1 9.8 %custom-call.29 = f32[1,128,128]{1,2,0:T(8,128)S(1)} custom-call(f32[1,128,128]{2,1,0:T(8,128)S(1)} %get-tuple-element.157), custom_call_target="InvertDiagBlocksLowerTriangular" | custom-call | tf_op jit(solution)/shard_map/jit(cholesky)/cholesky | solution.py:108
  223.3 11.7 %cholesky.343 = f32[128,128]{1,0:T(8,128)S(1)} custom-call(f32[128,128]{1,0:T(8,128)S(1)} %convolution_subtract_fusion.9), custom_call_target="Cholesky" | custom-call | tf_op jit(solution)/shard_map/jit(cholesky)/cholesky | solution.py:108
  241.2 10.9 %while.10 = (s32[]{:T(128)}, f32[512,512]{1,0:T(8,128)}, s32[4,2]{0,1:T(2,128)S(1)}, f32[4,128,128]{2,1,0:T(8,128)S(1)}, s32[]{:T(128)}) while((s32[]{:T(128)}, f32[512,512]{1,0:T(8,128)}, s32[4,2]{0,1:T(2,128)S(1)}, f32[4,128,128]{2,1,0:T(8,128)S(1)}, s32[]{:T(128)}) %tuple.98), condition=%wide.while_cond.4, body=%wide.while_body.4.sunk | while | flops 2 | bytes 131189 | solution.py:110
  252.1 39.3 %custom-call.30 = f32[4,128,128]{1,2,0:T(8,128)S(1)} custom-call(f32[4,128,128]{2,1,0:T(8,128)S(1)} %get-tuple-element.82), custom_call_target="InvertDiagBlocksLowerTriangular" | custom-call | tf_op jit(solution)/shard_map/triangular_solve/custom-call.3 | solution.py:110
  297.9 3.8 fusion.18
  307.0 3.9 pad_maximum_fusion
  313.8 3.3 copy.105
  317.1 4.0 select_select_fusion.3
  326.0 80.5 %all-reduce.8.cloned.1.call-done = f32[4,2,128,512]{3,2,0,1:T(8,128)} async-done(((f32[4,2,128,512]{3,2,0,1:T(8,128)}), f32[4,2,128,512]{3,2,0,1:T(8,128)}) %all-reduce.8.cloned.1.call-update) | async-done | bytes 2097168 | tf_op jit(solution)/shard_map/psum | solution.py:15
  406.5 5.8 negate_add_fusion.1
  413.9 101.5 %all-reduce.12.cloned.1.call-done = (f32[8,128,128]{1,2,0:T(8,128)}, f32[8,128,128]{1,2,0:T(8,128)}, f32[8,128,128]{1,2,0:T(8,128)}, f32[8,128,128]{1,2,0:T(8,128)}) async-done(((f32[8,128,128]{1,2,0:T(8,128)}, f32[8,128,128]{1,2,0:T(8,128)}, f32[8,128,128]{1,2,0:T(8,128)}, f32[8,128,128]{1,2,0:T(8,128)}), (f32[8,128,128]{1,2,0:T(8,128)}, f32[8,128,128]{1,2,0:T(8,128)}, f32[8,128,128]{1,2,0:T(8,128)}, ...) | async-done | bytes 2097168 | tf_op jit(solution)/shard_map/psum | solution.py:15
  522.4 4.8 collective-permute-done.7
  545.0 4.1 collective-permute-done.13
  556.1 11.7 %cholesky.358 = f32[128,128]{1,0:T(8,128)S(1)} custom-call(f32[128,128]{1,0:T(8,128)S(1)} %cholesky.439), custom_call_target="Cholesky" | custom-call | tf_op jit(solution)/shard_map/jit(cholesky)/cholesky | solution.py:108
  568.0 9.8 %custom-call.31 = f32[1,128,128]{1,2,0:T(8,128)S(1)} custom-call(f32[1,128,128]{2,1,0:T(8,128)S(1)} %get-tuple-element.153), custom_call_target="InvertDiagBlocksLowerTriangular" | custom-call | tf_op jit(solution)/shard_map/jit(cholesky)/cholesky | solution.py:108
  580.3 11.7 %cholesky.377 = f32[128,128]{1,0:T(8,128)S(1)} custom-call(f32[128,128]{1,0:T(8,128)S(1)} %cholesky.443), custom_call_target="Cholesky" | custom-call | tf_op jit(solution)/shard_map/jit(cholesky)/cholesky | solution.py:108
  592.1 10.0 %custom-call.32 = f32[1,128,128]{1,2,0:T(8,128)S(1)} custom-call(f32[1,128,128]{2,1,0:T(8,128)S(1)} %get-tuple-element.150), custom_call_target="InvertDiagBlocksLowerTriangular" | custom-call | tf_op jit(solution)/shard_map/jit(cholesky)/cholesky | solution.py:108
  603.6 11.7 %cholesky.398 = f32[128,128]{1,0:T(8,128)S(1)} custom-call(f32[128,128]{1,0:T(8,128)S(1)} %cholesky.448), custom_call_target="Cholesky" | custom-call | tf_op jit(solution)/shard_map/jit(cholesky)/cholesky | solution.py:108
  615.4 9.8 %custom-call.33 = f32[1,128,128]{1,2,0:T(8,128)S(1)} custom-call(f32[1,128,128]{2,1,0:T(8,128)S(1)} %get-tuple-element.147), custom_call_target="InvertDiagBlocksLowerTriangular" | custom-call | tf_op jit(solution)/shard_map/jit(cholesky)/cholesky | solution.py:108
  626.7 11.7 %cholesky.415 = f32[128,128]{1,0:T(8,128)S(1)} custom-call(f32[128,128]{1,0:T(8,128)S(1)} %convolution_subtract_fusion.8), custom_call_target="Cholesky" | custom-call | tf_op jit(solution)/shard_map/jit(cholesky)/cholesky | solution.py:108
  645.6 11.7 %while.11 = (s32[]{:T(128)}, f32[512,512]{1,0:T(8,128)}, s32[4,2]{0,1:T(2,128)S(1)}, f32[4,128,128]{2,1,0:T(8,128)S(1)}, s32[]{:T(128)}) while((s32[]{:T(128)}, f32[512,512]{1,0:T(8,128)}, s32[4,2]{0,1:T(2,128)S(1)}, f32[4,128,128]{2,1,0:T(8,128)S(1)}, s32[]{:T(128)}) %tuple.114), condition=%wide.while_cond.4.clone, body=%wide.while_body.4.clone.sunk | while | flops 2 | bytes 131189 | solution.py:110
  657.3 39.3 %custom-call.34 = f32[4,128,128]{1,2,0:T(8,128)S(1)} custom-call(f32[4,128,128]{2,1,0:T(8,128)S(1)} %get-tuple-element.83), custom_call_target="InvertDiagBlocksLowerTriangular" | custom-call | tf_op jit(solution)/shard_map/triangular_solve/custom-call.3 | solution.py:110
  704.5 3.8 fusion.15
  716.1 4.8 pad_maximum_fusion.1
  723.8 3.1 copy.115
  726.9 4.0 select_select_fusion
  735.1 11.9 %all-to-all-start.1 = ((s32[16,1,1]{2,1,0:T(1,128)}), s32[16,1,1]{2,1,0:T(1,128)S(1)}, u32[]{:S(2)}, u32[]{:S(2)}) async-start(s32[16,1,1]{2,1,0:T(1,128)} %copy.121), calls=%async_computation.1 | async-start | bytes 16384 | tf_op jit(solution)/shard_map/all_to_all | solution.py:178
  751.7 64.7 %all-reduce.10.cloned.1.call-done = f32[4,2,128,512]{3,2,0,1:T(8,128)} async-done(((f32[4,2,128,512]{3,2,0,1:T(8,128)}), f32[4,2,128,512]{3,2,0,1:T(8,128)}) %all-reduce.10.cloned.1.call-update) | async-done | bytes 2097168 | tf_op jit(solution)/shard_map/psum | solution.py:15
  816.4 5.6 negate_add_fusion
  824.1 3.1 copy.119
  827.3 3.9 reshape.731
  831.2 3.5 convolution_bitcast_fusion
  834.7 6.3 copy.120
  840.9 8.6 all-to-all-start
  850.3 3.6 copy.123
  853.9 88.3 %all-to-all-done = f32[16,1,65536]{2,1,0:T(1,128)} async-done(((f32[16,1,65536]{2,1,0:T(1,128)}), f32[16,1,65536]{2,1,0:T(1,128)}, u32[]{:S(2)}, u32[]{:S(2)}) %all-to-all-start) | async-done | bytes 4194336 | tf_op jit(solution)/shard_map/all_to_all | solution.py:177
  942.2 7.8 convolution_bitcast_fusion.1
  950.0 3.1 reshape.733
  (230 shorter events, 151.1 us)
Async XLA Ops:
  7.2 109.8 %all-reduce.14.cloned.1.call-start = ((), (), s32[]{:S(2)}) async-start(), calls=%async_computation.5 | async-start | bytes 4194304 | tf_op jit(solution)/shard_map/psum | solution.py:15
  11.8 2.0 copy-start
  13.8 392.8 %all-reduce.8.cloned.1.call-start = ((), (), s32[]{:S(2)}) async-start(), calls=%async_computation.2 | async-start | bytes 4194304 | tf_op jit(solution)/shard_map/psum | solution.py:15
  117.0 2.3 copy-start.14
  117.0 2.3 copy-start.13
  119.3 1.3 copy-start.4
  120.7 8.0 collective-permute-start
  122.0 6.7 collective-permute-start.1
  128.7 6.9 collective-permute-start.2
  128.7 6.9 collective-permute-start.3
  135.6 6.4 collective-permute-start.4
  135.7 6.9 collective-permute-start.5
  142.0 6.9 collective-permute-start.6
  151.8 1.0 copy-start.8
  239.6 51.8 %copy-start.2 = (f32[8,128,512]{2,1,0:T(8,128)S(1)}, f32[8,128,512]{2,1,0:T(8,128)}, u32[]{:S(2)}) copy-start(f32[8,128,512]{2,1,0:T(8,128)} %copy.102) | copy-start | bytes 6291460
  297.9 3.8 copy-start.7
  313.8 3.3 copy-start.12
  324.1 191.3 %all-reduce.12.cloned.1.call-start = ((), (), s32[]{:S(2)}) async-start(), calls=%async_computation.4 | async-start | bytes 4194304 | tf_op jit(solution)/shard_map/psum | solution.py:15
  413.7 402.7 %all-reduce.10.cloned.1.call-start = ((), (), s32[]{:S(2)}) async-start(), calls=%async_computation.3 | async-start | bytes 4194304 | tf_op jit(solution)/shard_map/psum | solution.py:15
  515.4 2.3 copy-start.16
  515.4 2.3 copy-start.15
  516.6 10.6 %copy-start.17 = (s32[2,56]{1,0:T(2,128)S(1)}, s32[2,56]{1,0:T(2,128)}, u32[]{:S(2)}) copy-start(s32[2,56]{1,0:T(2,128)} %param.21) | copy-start | bytes 1348
  517.8 1.3 copy-start.5
  519.1 8.0 collective-permute-start.7
  520.5 6.7 collective-permute-start.8
  527.1 8.9 collective-permute-start.9
  527.2 10.4 %collective-permute-start.10 = (f32[128,512]{0,1:T(8,128)S(1)}, f32[128,512]{0,1:T(8,128)S(1)}, u32[]{:S(2)}, u32[]{:S(2)}) collective-permute-start(f32[128,512]{0,1:T(8,128)S(1)} %collective-permute-done.8), channel_id=1, source_target_pairs={{0,112},{16,0},{32,16},{48,32},{64,48},{80,64},{96,80},{112,96},{1... | collective-permute-start | bytes 786440 | tf_op jit(solution)/shard_map/ppermute | solution.py:102
  536.1 6.4 collective-permute-start.11
  537.6 6.6 collective-permute-start.12
  542.5 6.6 collective-permute-start.13
  555.1 1.0 copy-start.9
  696.6 4.6 copy-start.1
  704.5 3.8 copy-start.6
  723.8 3.1 copy-start.11
  735.1 105.8 %all-to-all-start.1 = ((s32[16,1,1]{2,1,0:T(1,128)}), s32[16,1,1]{2,1,0:T(1,128)S(1)}, u32[]{:S(2)}, u32[]{:S(2)}) async-start(s32[16,1,1]{2,1,0:T(1,128)} %copy.121), calls=%async_computation.1 | async-start | bytes 16384 | tf_op jit(solution)/shard_map/all_to_all | solution.py:178
  816.4 5.7 copy-start.3
  840.9 101.2 %all-to-all-start = ((f32[16,1,65536]{2,1,0:T(1,128)}), f32[16,1,65536]{2,1,0:T(1,128)}, u32[]{:S(2)}, u32[]{:S(2)}) async-start(f32[16,1,65536]{2,1,0:T(1,128)} %copy.120), calls=%async_computation | async-start | bytes 8388608 | tf_op jit(solution)/shard_map/all_to_all | solution.py:177
  950.0 3.1 copy-start.10
Sparse Core Ops, SparseCore 0:
  13.5 103.4 all-reduce.13
  324.2 82.2 all-reduce.7
  413.9 101.4 all-reduce.11
  734.0 82.4 all-reduce.9
